TPU v7x, 256 devices: a whole 4x4x8 slice. The times are simulated.
256 devices in a mesh: row: 16 (over z, core), col: 16 (over y, x).
Axes of the slice: x: 4, y: 4, z: 8, core: 2. Of those that a mesh axis runs over, the one named last changes fastest.
Arguments:
- matrix: bfloat16 [4096, 262144], P('row', 'col'), may hold values from -60 to 60
- test_matrix: bfloat16 [262144, 512], P(('col', 'row')), may hold values from -0.0390625 to 0.0390625
Outputs:
- orthonormal: float32 [4096, 512], P(('row', 'col'))
- triangular: float32 [512, 512], replicated
All inputs are finite; a program needn't handle non-finite values.
Results may differ from a plain program's by a relative error of at most 0.0003.
Values may be sent and summed in bfloat16 or wider, within the bound.
No kernel may reach another device: no remote copies, remote signals or barrier semaphores. Data moves between devices by JAX's collectives and lax.ppermute only.
A program may use at most 128 MiB of HBM per device.

v0:
```python
import jax
import jax.numpy as jnp
from jax import lax
from jax.sharding import PartitionSpec as P


def probe_product(matrix, test_matrix):
    return jnp.dot(
        matrix,
        lax.all_gather(test_matrix, "row", axis=0, tiled=True),
        preferred_element_type=jnp.float32,
    )


def scatter_sum(value, axis, parts):
    pieces = value.reshape(parts, value.shape[0] // parts, *value.shape[1:])
    return lax.all_to_all(pieces, axis, 0, 0, tiled=False).sum(0)


def gather_rows(value, axis, parts):
    copies = jnp.broadcast_to(value[None], (parts, *value.shape))
    gathered = lax.all_to_all(copies, axis, 0, 0, tiled=False)
    return gathered.reshape(parts * value.shape[0], *value.shape[1:])


def shards(matrix, test_matrix):
    n_col = lax.axis_size("col")
    n_row = lax.axis_size("row")
    total_rows = matrix.shape[0] * n_row
    k = test_matrix.shape[1]
    partial_value = probe_product(matrix, test_matrix)
    own_rows = scatter_sum(partial_value, "col", n_col)
    sketch = gather_rows(own_rows, "col", n_col)
    width = k // n_col
    col = lax.axis_index("col")
    columns = lax.dynamic_slice_in_dim(sketch, col * width, width, 1)
    gram_part = jnp.dot(sketch.T, columns, precision=lax.Precision.HIGHEST)
    gram_part = gather_rows(scatter_sum(gram_part, "row", n_row), "row", n_row)
    blocks = gather_rows(gram_part.T, "col", n_col)
    gram = blocks.T / jnp.float32(total_rows)
    lower_factor = jnp.linalg.cholesky(gram)
    orthonormal = lax.linalg.triangular_solve(
        lower_factor, own_rows, left_side=False, lower=True, transpose_a=True
    )
    return (orthonormal, lower_factor.T)


def solution(mesh):
    in_specs = (P("row", "col"), P(("col", "row"), None))
    out_specs = (P(("row", "col"), None), P())
    return jax.shard_map(shards, mesh=mesh, in_specs=in_specs, out_specs=out_specs, check_vma=False)
```

profile of v0, /device:TPU:1, one launch (start us, length us, event | category | flops | bytes accessed | tf_op | source)
XLA Modules:
  0.0 345.5 jit_solution(3495870859918004758)
XLA Ops:
  7.9 101.5 %all-gather.2.cloned.1.call-done = bf16[16384,512]{1,0:T(8,128)(2,1)} async-done(((bf16[1024,512]{1,0:T(8,128)(2,1)}), bf16[16384,512]{1,0:T(8,128)(2,1)}) %all-gather.2.cloned.1.call-update) | async-done | bytes 16777232 | tf_op jit(solution)/shard_map/all_gather | solution.py:10
  109.4 10.5 %fusion.37 = f32[256,512]{1,0:T(8,128)S(1)} fusion(bf16[256,16384]{1,0:T(8,128)(2,1)} %param.2, bf16[16384,512]{1,0:T(8,128)(2,1)} %all-gather.2.cloned.1.call-done), kind=kOutput, calls=%fused_computation.74 | convolution fusion | flops 4294967296 | bytes 25690112 | tf_op jit(solution)/shard_map/dot_general | solution.py:8
  119.9 17.2 %all_to_all.25 = f32[16,16,512]{2,1,0:T(8,128)S(1)} all-to-all(f32[16,16,512]{2,1,0:T(8,128)S(1)} %bitcast.75), channel_id=1, replica_groups=mesh['row'=16,'col'=16] {'col'}, dimensions={0} | all-to-all | bytes 1048576 | tf_op jit(solution)/shard_map/all_to_all | solution.py:17
  138.0 3.6 %all-to-all-start.1 = ((f32[16,16,512]{2,1,0:T(8,128)}), f32[16,16,512]{2,1,0:T(8,128)S(1)}, u32[]{:S(2)}, u32[]{:S(2)}) async-start(f32[16,16,512]{2,1,0:T(8,128)} %broadcast_in_dim.7), calls=%async_computation.1 | async-start | bytes 1048576 | tf_op jit(solution)/shard_map/all_to_all | solution.py:22
  141.5 10.1 %all-to-all-done.1 = f32[16,16,512]{2,1,0:T(8,128)S(1)} async-done(((f32[16,16,512]{2,1,0:T(8,128)}), f32[16,16,512]{2,1,0:T(8,128)S(1)}, u32[]{:S(2)}, u32[]{:S(2)}) %all-to-all-start.1) | async-done | bytes 524320 | tf_op jit(solution)/shard_map/all_to_all | solution.py:22
  152.7 14.2 %all_to_all.26 = f32[16,1,1024]{2,1,0:T(1,128)S(1)} all-to-all(f32[16,1,1024]{2,1,0:T(1,128)S(1)} %reshape.80), channel_id=1, replica_groups=mesh['row'=16,'col'=16] {'row'}, dimensions={0} | all-to-all | bytes 131072 | tf_op jit(solution)/shard_map/all_to_all | solution.py:17
  168.6 10.3 %all_to_all.27 = f32[16,1,1024]{2,1,0:T(1,128)S(1)} all-to-all(f32[16,1,1024]{2,1,0:T(1,128)S(1)} %reshape.82), channel_id=1, replica_groups=mesh['row'=16,'col'=16] {'row'}, dimensions={0} | all-to-all | bytes 131072 | tf_op jit(solution)/shard_map/all_to_all | solution.py:22
  180.2 1.1 broadcast_in_dim.9
  181.3 3.8 %all-to-all-start.4 = ((f32[16,32,512]{2,1,0:T(8,128)}), f32[16,32,512]{2,1,0:T(8,128)S(1)}, u32[]{:S(2)}, u32[]{:S(2)}) async-start(f32[16,32,512]{2,1,0:T(8,128)} %broadcast_in_dim.9), calls=%async_computation.4 | async-start | bytes 2097152 | tf_op jit(solution)/shard_map/all_to_all | solution.py:22
  185.1 18.0 %all-to-all-done.4 = f32[16,32,512]{2,1,0:T(8,128)S(1)} async-done(((f32[16,32,512]{2,1,0:T(8,128)}), f32[16,32,512]{2,1,0:T(8,128)S(1)}, u32[]{:S(2)}, u32[]{:S(2)}) %all-to-all-start.4) | async-done | bytes 1048608 | tf_op jit(solution)/shard_map/all_to_all | solution.py:22
  203.7 11.7 %cholesky.104 = f32[128,128]{1,0:T(8,128)S(1)} custom-call(f32[128,128]{1,0:T(8,128)S(1)} %cholesky.266), custom_call_target="Cholesky" | custom-call | tf_op jit(solution)/shard_map/jit(cholesky)/cholesky | solution.py:41
  215.6 9.8 %custom-call.30 = f32[1,128,128]{1,2,0:T(8,128)S(1)} custom-call(f32[1,128,128]{2,1,0:T(8,128)S(1)} %get-tuple-element.39), custom_call_target="InvertDiagBlocksLowerTriangular" | custom-call | tf_op jit(solution)/shard_map/jit(cholesky)/cholesky | solution.py:41
  226.1 11.7 %cholesky.217 = f32[128,128]{1,0:T(8,128)S(1)} custom-call(f32[128,128]{1,0:T(8,128)S(1)} %cholesky.270), custom_call_target="Cholesky" | custom-call | tf_op jit(solution)/shard_map/jit(cholesky)/cholesky | solution.py:41
  237.8 10.0 %custom-call.31 = f32[1,128,128]{1,2,0:T(8,128)S(1)} custom-call(f32[1,128,128]{2,1,0:T(8,128)S(1)} %get-tuple-element.36), custom_call_target="InvertDiagBlocksLowerTriangular" | custom-call | tf_op jit(solution)/shard_map/jit(cholesky)/cholesky | solution.py:41
  248.5 11.7 %cholesky.238 = f32[128,128]{1,0:T(8,128)S(1)} custom-call(f32[128,128]{1,0:T(8,128)S(1)} %cholesky.275), custom_call_target="Cholesky" | custom-call | tf_op jit(solution)/shard_map/jit(cholesky)/cholesky | solution.py:41
  260.2 9.8 %custom-call.32 = f32[1,128,128]{1,2,0:T(8,128)S(1)} custom-call(f32[1,128,128]{2,1,0:T(8,128)S(1)} %get-tuple-element.33), custom_call_target="InvertDiagBlocksLowerTriangular" | custom-call | tf_op jit(solution)/shard_map/jit(cholesky)/cholesky | solution.py:41
  270.7 11.7 %cholesky.255 = f32[128,128]{1,0:T(8,128)S(1)} custom-call(f32[128,128]{1,0:T(8,128)S(1)} %convolution_subtract_fusion.2), custom_call_target="Cholesky" | custom-call | tf_op jit(solution)/shard_map/jit(cholesky)/cholesky | solution.py:41
  287.5 8.5 %while.1 = (s32[]{:T(128)}, f32[512,512]{1,0:T(8,128)S(1)}, s32[4,2]{0,1:T(2,128)S(1)}, f32[4,128,128]{2,1,0:T(8,128)S(1)}, s32[]{:T(128)}) while((s32[]{:T(128)}, f32[512,512]{1,0:T(8,128)S(1)}, s32[4,2]{0,1:T(2,128)S(1)}, f32[4,128,128]{2,1,0:T(8,128)S(1)}, s32[]{:T(128)}) %tuple.36), condition=%wide.while_cond, body=%wide.while_body.sunk | while | flops 2 | bytes 131189 | solution.py:42
  288.2 1.4 bitcast_dynamic-update-slice_fusion.2
  290.3 1.4 bitcast_dynamic-update-slice_fusion.2
  292.4 1.4 bitcast_dynamic-update-slice_fusion.2
  294.5 1.4 bitcast_dynamic-update-slice_fusion.2
  296.0 39.3 %custom-call.33 = f32[4,128,128]{1,2,0:T(8,128)S(1)} custom-call(f32[4,128,128]{2,1,0:T(8,128)S(1)} %get-tuple-element.9), custom_call_target="InvertDiagBlocksLowerTriangular" | custom-call | tf_op jit(solution)/shard_map/triangular_solve | solution.py:42
  337.4 1.3 copy.20
  (57 shorter events, 15.6 us)
Async XLA Ops:
  7.2 102.2 %all-gather.2.cloned.1.call-start = ((), (), s32[]{:S(2)}) async-start(), calls=%async_computation.5 | async-start | bytes 17825792 | tf_op jit(solution)/shard_map/all_gather | solution.py:10
  138.0 13.7 %all-to-all-start.1 = ((f32[16,16,512]{2,1,0:T(8,128)}), f32[16,16,512]{2,1,0:T(8,128)S(1)}, u32[]{:S(2)}, u32[]{:S(2)}) async-start(f32[16,16,512]{2,1,0:T(8,128)} %broadcast_in_dim.7), calls=%async_computation.1 | async-start | bytes 1048576 | tf_op jit(solution)/shard_map/all_to_all | solution.py:22
  181.3 21.8 %all-to-all-start.4 = ((f32[16,32,512]{2,1,0:T(8,128)}), f32[16,32,512]{2,1,0:T(8,128)S(1)}, u32[]{:S(2)}, u32[]{:S(2)}) async-start(f32[16,32,512]{2,1,0:T(8,128)} %broadcast_in_dim.9), calls=%async_computation.4 | async-start | bytes 2097152 | tf_op jit(solution)/shard_map/all_to_all | solution.py:22
Sparse Core Ops, SparseCore 0:
  9.8 99.5 all-gather.1
where the time goes:
time: 346 us
  waiting for transfers between devices  130 us (38%)
  other arithmetic  121 us (35%)
  blocking collectives  41.7 us (12%)
  between operations  16.8 us (5%)
  matrix products  14.5 us (4%)
  local copies, waits for them, and re-layouts  13.8 us (4%)
  starting transfers between devices  7.45 us (2%)
    all_gather x1, waiting for transfers between devices, probe_product(): lax.all_gather(test_matrix, 'row', axis=0, tiled=True)  101 us
    another operation x14, other arithmetic, shards(): lower_factor = jnp.linalg.cholesky(gram)  78.6 us
    another operation x3, other arithmetic, shards(): lax.linalg.triangular_solve(lower_factor, own_rows, left_side=False, lowe...  40 us
    all_to_all x2, blocking collectives, scatter_sum(): return lax.all_to_all(pieces, axis, 0, 0, tiled=False).sum(0)  31.4 us
    all_to_all x2, waiting for transfers between devices, gather_rows(): gathered = lax.all_to_all(copies, axis, 0, 0, tiled=False)  28.1 us
    dot_general x1, matrix products, probe_product(): jnp.dot(matrix, lax.all_gather(test_matrix, 'row', axis=0, tiled=True), p...  10.5 us
    all_to_all x1, blocking collectives, gather_rows(): gathered = lax.all_to_all(copies, axis, 0, 0, tiled=False)  10.3 us
    another operation x12, local copies, waits for them, and re-layouts  8.39 us
  transfers between devices with their start and end apart: 3, of which 3 were waited for; matrix products, arithmetic and copies ran while one was open for 0% of the time, Pallas kernels for 0%

commit v1 on v0

--- a/solution.py
+++ b/solution.py
@@ -5,11 +5,16 @@
 
 
 def probe_product(matrix, test_matrix):
-    return jnp.dot(
-        matrix,
-        lax.all_gather(test_matrix, "row", axis=0, tiled=True),
-        preferred_element_type=jnp.float32,
-    )
+
+    def paths_create(dim_at, mesh_name, z):
+        return jnp.concatenate(
+            jax.lax.all_to_all(
+                jnp.stack(tuple((z for _ in range(jax.lax.axis_size(mesh_name))))), mesh_name, 0, 0
+            ),
+            dim_at,
+        )
+
+    return jnp.dot(matrix, paths_create(0, "row", test_matrix), preferred_element_type=jnp.float32)
 
 
 def scatter_sum(value, axis, parts):

time: 346 us -> 606 us (1.75)
  blocking collectives: 41.7 us -> 415 us
  waiting for transfers between devices: 130 us -> 28.9 us
  between operations: 16.8 us -> 3.44 us
    all_to_all x0 -> x1, blocking collectives: none -> 375 us  [paths_create(): jax.lax.all_to_all(jnp.stack(tuple((z for _ in range(jax.lax.axis_size(me...]
    all_gather x1 -> x0, waiting for transfers between devices: 101 us -> none  [probe_product(): lax.all_gather(test_matrix, 'row', axis=0, tiled=True)]
  transfers between devices with their start and end apart: 3 -> 2, of which waited for: 3 -> 2; matrix products, arithmetic and copies ran while one was open for 0% -> 0% of each run, Pallas kernels for 0% -> 0%
where the time goes in v1:
time: 606 us; the launch traced here: 605 us
  blocking collectives  415 us (68%)
  other arithmetic  121 us (20%)
  waiting for transfers between devices  28.9 us (5%)
  local copies, waits for them, and re-layouts  17.4 us (3%)
  matrix products  11.4 us (2%)
  starting transfers between devices  7.41 us (1%)
    all_to_all x1, blocking collectives, paths_create(): jax.lax.all_to_all(jnp.stack(tuple((z for _ in range(jax.lax.axis_size(me...  375 us
    another operation x14, other arithmetic, shards(): lower_factor = jnp.linalg.cholesky(gram)  78.6 us
    another operation x3, other arithmetic, shards(): lax.linalg.triangular_solve(lower_factor, own_rows, left_side=False, lowe...  40 us
    all_to_all x2, blocking collectives, scatter_sum(): return lax.all_to_all(pieces, axis, 0, 0, tiled=False).sum(0)  29.6 us
    all_to_all x2, waiting for transfers between devices, gather_rows(): gathered = lax.all_to_all(copies, axis, 0, 0, tiled=False)  28.9 us
  transfers between devices with their start and end apart: 2, of which 2 were waited for; matrix products, arithmetic and copies ran while one was open for 0% of the time, Pallas kernels for 0%

profile of v1, /device:TPU:1, one launch (start us, length us, event | category | flops | bytes accessed | tf_op | source)
XLA Modules:
  0.0 604.9 jit_solution(7362938672495359985)
XLA Ops:
  0.6 3.6 stack.2
  4.3 375.3 %all_to_all.30 = bf16[16,1024,512]{2,1,0:T(8,128)(2,1)S(1)} all-to-all(bf16[16,1024,512]{2,1,0:T(8,128)(2,1)S(1)} %stack.2), channel_id=1, replica_groups=mesh['row'=16,'col'=16] {'row'}, dimensions={0} | all-to-all | bytes 33554432 | tf_op jit(solution)/shard_map/all_to_all | solution.py:11
  379.5 7.4 %fusion.37 = f32[16,16,512]{2,1,0:T(8,128)S(1)} fusion(bf16[16,16,16384]{2,1,0:T(8,128)(2,1)} %bitcast.80, bf16[16384,512,1]{1,0,2:T(8,128)(2,1)S(1)} %bitcast.73), kind=kOutput, calls=%fused_computation.74 | convolution fusion | flops 4294967296 | bytes 25690112 | tf_op jit(solution)/shard_map/dot_general | solution.py:17
  386.9 17.9 %all_to_all.31 = f32[16,16,512]{2,1,0:T(8,128)S(1)} all-to-all(f32[16,16,512]{2,1,0:T(8,128)S(1)} %fusion.37), channel_id=1, replica_groups=mesh['row'=16,'col'=16] {'col'}, dimensions={0} | all-to-all | bytes 1048576 | tf_op jit(solution)/shard_map/all_to_all | solution.py:22
  405.8 3.6 all-to-all-start.2
  409.4 11.0 %all-to-all-done.2 = f32[16,16,512]{2,1,0:T(8,128)S(1)} async-done(((f32[16,16,512]{2,1,0:T(8,128)}), f32[16,16,512]{2,1,0:T(8,128)S(1)}, u32[]{:S(2)}, u32[]{:S(2)}) %all-to-all-start.2) | async-done | bytes 524320 | tf_op jit(solution)/shard_map/all_to_all | solution.py:27
  421.3 11.7 %all_to_all.32 = f32[16,1,1024]{2,1,0:T(1,128)S(1)} all-to-all(f32[16,1,1024]{2,1,0:T(1,128)S(1)} %reshape.85), channel_id=1, replica_groups=mesh['row'=16,'col'=16] {'row'}, dimensions={0} | all-to-all | bytes 131072 | tf_op jit(solution)/shard_map/all_to_all | solution.py:22
  434.8 10.4 %all_to_all.33 = f32[16,1,1024]{2,1,0:T(1,128)S(1)} all-to-all(f32[16,1,1024]{2,1,0:T(1,128)S(1)} %reshape.87), channel_id=1, replica_groups=mesh['row'=16,'col'=16] {'row'}, dimensions={0} | all-to-all | bytes 131072 | tf_op jit(solution)/shard_map/all_to_all | solution.py:27
  447.5 3.8 all-to-all-start.5
  451.4 18.0 %all-to-all-done.5 = f32[16,32,512]{2,1,0:T(8,128)S(1)} async-done(((f32[16,32,512]{2,1,0:T(8,128)}), f32[16,32,512]{2,1,0:T(8,128)S(1)}, u32[]{:S(2)}, u32[]{:S(2)}) %all-to-all-start.5) | async-done | bytes 1048608 | tf_op jit(solution)/shard_map/all_to_all | solution.py:27
  470.0 11.7 %cholesky.104 = f32[128,128]{1,0:T(8,128)S(1)} custom-call(f32[128,128]{1,0:T(8,128)S(1)} %cholesky.266), custom_call_target="Cholesky" | custom-call | tf_op jit(solution)/shard_map/jit(cholesky)/cholesky | solution.py:46
  481.8 9.8 %custom-call.30 = f32[1,128,128]{1,2,0:T(8,128)S(1)} custom-call(f32[1,128,128]{2,1,0:T(8,128)S(1)} %get-tuple-element.39), custom_call_target="InvertDiagBlocksLowerTriangular" | custom-call | tf_op jit(solution)/shard_map/jit(cholesky)/cholesky | solution.py:46
  492.3 11.7 %cholesky.217 = f32[128,128]{1,0:T(8,128)S(1)} custom-call(f32[128,128]{1,0:T(8,128)S(1)} %cholesky.270), custom_call_target="Cholesky" | custom-call | tf_op jit(solution)/shard_map/jit(cholesky)/cholesky | solution.py:46
  504.1 10.0 %custom-call.31 = f32[1,128,128]{1,2,0:T(8,128)S(1)} custom-call(f32[1,128,128]{2,1,0:T(8,128)S(1)} %get-tuple-element.36), custom_call_target="InvertDiagBlocksLowerTriangular" | custom-call | tf_op jit(solution)/shard_map/jit(cholesky)/cholesky | solution.py:46
  514.7 11.7 %cholesky.238 = f32[128,128]{1,0:T(8,128)S(1)} custom-call(f32[128,128]{1,0:T(8,128)S(1)} %cholesky.275), custom_call_target="Cholesky" | custom-call | tf_op jit(solution)/shard_map/jit(cholesky)/cholesky | solution.py:46
  526.5 9.8 %custom-call.32 = f32[1,128,128]{1,2,0:T(8,128)S(1)} custom-call(f32[1,128,128]{2,1,0:T(8,128)S(1)} %get-tuple-element.33), custom_call_target="InvertDiagBlocksLowerTriangular" | custom-call | tf_op jit(solution)/shard_map/jit(cholesky)/cholesky | solution.py:46
  536.9 11.7 %cholesky.255 = f32[128,128]{1,0:T(8,128)S(1)} custom-call(f32[128,128]{1,0:T(8,128)S(1)} %convolution_subtract_fusion.2), custom_call_target="Cholesky" | custom-call | tf_op jit(solution)/shard_map/jit(cholesky)/cholesky | solution.py:46
  553.7 8.5 %while.1 = (s32[]{:T(128)}, f32[512,512]{1,0:T(8,128)S(1)}, s32[4,2]{0,1:T(2,128)S(1)}, f32[4,128,128]{2,1,0:T(8,128)S(1)}, s32[]{:T(128)}) while((s32[]{:T(128)}, f32[512,512]{1,0:T(8,128)S(1)}, s32[4,2]{0,1:T(2,128)S(1)}, f32[4,128,128]{2,1,0:T(8,128)S(1)}, s32[]{:T(128)}) %tuple.36), condition=%wide.while_cond, body=%wide.while_body.sunk | while | flops 2 | bytes 131189 | solution.py:47
  554.4 1.4 bitcast_dynamic-update-slice_fusion.2
  556.5 1.4 bitcast_dynamic-update-slice_fusion.2
  558.7 1.4 bitcast_dynamic-update-slice_fusion.2
  560.8 1.4 bitcast_dynamic-update-slice_fusion.2
  562.2 39.3 %custom-call.33 = f32[4,128,128]{1,2,0:T(8,128)S(1)} custom-call(f32[4,128,128]{2,1,0:T(8,128)S(1)} %get-tuple-element.9), custom_call_target="InvertDiagBlocksLowerTriangular" | custom-call | tf_op jit(solution)/shard_map/triangular_solve | solution.py:47
  603.6 1.3 copy.20
  (56 shorter events, 15.9 us)
Async XLA Ops:
  405.8 14.5 %all-to-all-start.2 = ((f32[16,16,512]{2,1,0:T(8,128)}), f32[16,16,512]{2,1,0:T(8,128)S(1)}, u32[]{:S(2)}, u32[]{:S(2)}) async-start(f32[16,16,512]{2,1,0:T(8,128)} %broadcast_in_dim.7), calls=%async_computation.2 | async-start | bytes 1048576 | tf_op jit(solution)/shard_map/all_to_all | solution.py:27
  447.5 21.8 %all-to-all-start.5 = ((f32[16,32,512]{2,1,0:T(8,128)}), f32[16,32,512]{2,1,0:T(8,128)S(1)}, u32[]{:S(2)}, u32[]{:S(2)}) async-start(f32[16,32,512]{2,1,0:T(8,128)} %broadcast_in_dim.9), calls=%async_computation.5 | async-start | bytes 2097152 | tf_op jit(solution)/shard_map/all_to_all | solution.py:27
